TPU v7x, 32 devices: a whole 2x2x4 slice. The times are simulated.
32 devices in a mesh: chain: 8 (over z, x), grp: 4 (over y, core).
Axes of the slice: x: 2, y: 2, z: 4, core: 2. Of those that a mesh axis runs over, the one named last changes fastest.
Arguments:
- right_side: float32 [16, 4, 64, 128], P('chain', 'grp'), may hold values from -0.8 to 0.8
- factor: float32 [16, 4, 2, 128, 128], P('chain', 'grp'), may hold values from -1 to 1
- inverse_diag: float32 [16, 4, 128, 128], P('chain', 'grp'), as said below
- pattern: int32 [16, 4, 2], P('chain'), may hold values from 0 to 3, as said below
Outputs:
- forward_result: float32 [16, 4, 64, 128], P('chain', 'grp')
- solution: float32 [16, 4, 64, 128], P('chain', 'grp')
Inputs may be any that keep to these rules, and one draw needn't show every extreme that they name: `pattern`: the 2 entries of one supernode are different supernodes of the previous level. `inverse_diag`: every block is lower triangular with a diagonal between 0.75 and 1.05.
All inputs are finite; a program needn't handle non-finite values.
Results may differ from a plain program's by a relative error of at most 0.0002.
Values sent between devices are 32-bit elements; how exact they have to be, the bound alone decides.
No kernel may reach another device: no remote copies, remote signals or barrier semaphores. Data moves between devices by JAX's collectives and lax.ppermute only.
A program may use at most 320 MiB of HBM per device.

v0:
```python
import jax
import jax.numpy as jnp
from jax import lax
from jax.sharding import PartitionSpec as P

PRECISE = lax.Precision.HIGHEST


def carried_in(value, axis, join, neutral, backward):
    count, mine = (lax.axis_size(axis), lax.axis_index(axis))
    pieces = jax.tree.map(lambda part: lax.all_gather(part, axis), value)
    if backward:
        pieces = jax.tree.map(lambda part: part[::-1], pieces)
        mine = count - 1 - mine
    subtotal = jax.tree.map(
        lambda part, zero: jnp.full_like(part, 0) + jnp.asarray(zero, part.dtype), value, neutral
    )

    def hop(position, subtotal):
        longer = join(subtotal, jax.tree.map(lambda part: part[position], pieces))
        return jax.tree.map(lambda new, old: jnp.where(position < mine, new, old), longer, subtotal)

    return lax.fori_loop(0, count - 1, hop, subtotal)


def matmul(left_side, right_factor):
    return jnp.dot(left_side, right_factor, precision=PRECISE, preferred_element_type=jnp.float32)


def matmul_trans(left_side, right_factor):
    return lax.dot_general(
        left_side,
        right_factor,
        (((1,), (1,)), ((), ())),
        precision=PRECISE,
        preferred_element_type=jnp.float32,
    )


def combine_forward(earlier_map, later_map):
    return (
        matmul(earlier_map[0], later_map[0]),
        matmul(earlier_map[1], later_map[0]) + later_map[1],
    )


def combine_backward(earlier_map, later_map):
    return (
        matmul(later_map[0], earlier_map[0]),
        matmul_trans(earlier_map[1], later_map[0]) + later_map[1],
    )


def fold_maps(running, inputs):
    return ((matmul(running[0], inputs[0]), matmul(running[1], inputs[0]) + inputs[1]), None)


def forward_step(previous, inputs):
    updated = matmul(previous, inputs[0]) + inputs[1]
    return (updated, updated)


def back_fold(running, inputs):
    return (matmul_trans(running - inputs[1], inputs[0]), None)


def shards(right_side, factor, inverse_diag, pattern):
    levels = right_side.shape[0]
    samples = right_side.shape[2]
    sup_rows = right_side.shape[3]
    groups = lax.axis_size("grp")
    level_rows = groups * sup_rows
    my_group = lax.axis_index("grp")
    scaled = jnp.einsum(
        "lgti,lgkij->lgktj",
        inverse_diag,
        factor,
        precision=PRECISE,
        preferred_element_type=jnp.float32,
    )
    lifted = jnp.einsum(
        "lgsi,lgti->lgst",
        right_side,
        inverse_diag,
        precision=PRECISE,
        preferred_element_type=jnp.float32,
    )
    blocks, offsets = (
        lax.all_gather(scaled, "grp", axis=1, tiled=True),
        lax.all_gather(lifted, "grp", axis=1, tiled=True),
    )
    onehot = (pattern[..., None] == jnp.arange(groups, dtype=jnp.int32)).astype(jnp.float32)
    level_maps = -jnp.einsum(
        "lgkh,lgktj->lhjgt", onehot, blocks, precision=PRECISE, preferred_element_type=jnp.float32
    )
    level_maps = level_maps.reshape(levels, level_rows, level_rows)
    sources = offsets.transpose(0, 2, 1, 3).reshape(levels, samples, level_rows)
    (total_map, total_shift), _ = lax.scan(
        fold_maps, (level_maps[0], sources[0]), (level_maps[1:], sources[1:])
    )
    neutral = (
        jnp.eye(level_rows, dtype=jnp.float32),
        jnp.zeros((samples, level_rows), jnp.float32),
    )
    _, incoming = carried_in((total_map, total_shift), "chain", combine_forward, neutral, False)
    _, solved = lax.scan(forward_step, incoming, (level_maps, sources))
    forward_own = lax.dynamic_slice_in_dim(solved, my_group * sup_rows, sup_rows, 2)
    back_shift, _ = lax.scan(
        back_fold, jnp.zeros((samples, level_rows), jnp.float32), (level_maps, solved), reverse=True
    )
    _, arriving = carried_in((total_map, back_shift), "chain", combine_backward, neutral, True)
    own_inverse = inverse_diag[:, 0]

    def back_step(running, inputs):
        level_map, forward_rows, inverse = inputs
        own_rows = lax.dynamic_slice_in_dim(forward_rows, my_group * sup_rows, sup_rows, 1)
        own_pending = lax.dynamic_slice_in_dim(running, my_group * sup_rows, sup_rows, 1)
        answer = matmul(own_rows - own_pending, inverse)
        return (matmul_trans(running - forward_rows, level_map), answer)

    _, answers = lax.scan(back_step, arriving, (level_maps, solved, own_inverse), reverse=True)
    return (forward_own[:, None], answers[:, None])


def solution(mesh):
    return jax.shard_map(
        shards,
        mesh=mesh,
        in_specs=(
            P("chain", "grp", None, None),
            P("chain", "grp", None, None, None),
            P("chain", "grp", None, None),
            P("chain", None, None),
        ),
        out_specs=(P("chain", "grp", None, None), P("chain", "grp", None, None)),
        check_vma=False,
    )
```

profile of v0, /device:TPU:0, one launch (start us, length us, event | category | flops | bytes accessed | tf_op | source)
XLA Modules:
  0.0 289.6 jit_solution(16148861564298682824)
XLA Ops:
  7.2 0.9 copy-done
  8.1 1.5 convolution_bitcast_fusion.4
  9.6 0.8 copy.22
  10.5 0.8 copy.23
  11.3 1.3 fusion.50
  12.6 7.2 %all-gather.1 = f32[2,256,128]{2,1,0:T(8,128)S(1)} all-gather(f32[2,64,128]{2,1,0:T(8,128)S(1)} %fusion.50), channel_id=3, replica_groups=mesh['chain'=8,'grp'=4] {'grp'}, dimensions={1}, use_global_device_ids=true | all-gather | bytes 327680 | tf_op jit(solution)/shard_map/all_gather | solution.py:90
  20.0 0.7 fusion.58
  20.8 9.2 %all-gather.9.cloned.1.call-done = f32[2,4,2,128,128]{4,3,2,0,1:T(8,128)} async-done(((f32[2,1,2,128,128]{4,3,2,0,1:T(8,128)}), f32[2,4,2,128,128]{4,3,2,0,1:T(8,128)}) %all-gather.9.cloned.1.call-update) | async-done | bytes 1048592 | tf_op jit(solution)/shard_map/all_gather | solution.py:89
  30.1 3.9 %negate_bitcast_fusion = f32[2,4,128,4,128]{2,1,4,3,0:T(4,128)S(1)} fusion(f32[2,4,2,128,128]{4,3,2,0,1:T(8,128)} %all-gather.9.cloned.1.call-done, s32[2,4,2]{2,1,0:T(4,128)S(1)} %copy.23), kind=kOutput, calls=%fused_computation.46 | convolution fusion | flops 13107264 | bytes 3145792 | tf_op jit(solution)/shard_map/lgkh,lgktj->lhjgt/dot_general | solution.py:93
  34.0 1.1 fusion.57
  35.1 1.8 convolution_add_fusion
  37.0 5.7 %fusion.39 = f32[512,512]{1,0:T(8,128)} fusion(f32[64,8,4,128]{3,2,1,0:T(4,128)} %bitcast.155, f32[64,8,4,128]{3,2,1,0:T(4,128)S(1)} %bitcast.154), kind=kOutput, calls=%fused_computation.50 | convolution fusion | flops 1610612736 | bytes 3145728 | tf_op jit(solution)/shard_map/while/body/eval_jaxpr/dot_general | solution.py:27
  42.9 1.1 reshape.43
  44.0 1.9 reshape.42
  45.9 1.9 copy.26
  47.8 29.5 %all-gather.13.cloned.1.call-done = f32[512,512]{1,0:T(8,128)} async-done(((f32[64,512]{1,0:T(8,128)}), f32[512,512]{1,0:T(8,128)}) %all-gather.13.cloned.1.call-update) | async-done | bytes 1048592 | tf_op jit(solution)/shard_map/all_gather | solution.py:11
  77.3 125.4 %all-gather.11.cloned.1.call-done = f32[4096,512]{1,0:T(8,128)} async-done(((f32[512,512]{1,0:T(8,128)}), f32[4096,512]{1,0:T(8,128)}) %all-gather.11.cloned.1.call-update) | async-done | bytes 8388624 | tf_op jit(solution)/shard_map/all_gather | solution.py:11
  202.7 14.4 %while.79 = (s32[]{:T(128)}, f32[64,512]{1,0:T(8,128)S(1)}, s32[]{:T(128)}, f32[8,512,512]{2,1,0:T(8,128)}, f32[8,64,512]{2,1,0:T(8,128)}, /*index=5*/s32[]{:T(128)}, s32[]{:T(128)}) while((s32[]{:T(128)}, f32[64,512]{1,0:T(8,128)S(1)}, s32[]{:T(128)}, f32[8,512,512]{2,1,0:T(8,128)}, f32[8,64,512]{2,1,0:T(8,128)}, ...), condition=%wide.region_1.2_spmd.clone, body=%wide.region_0.1_spmd.clone.sunk | while | flops 201457664 | bytes 1837671 | solution.py:23
  202.7 2.0 fusion.82
  204.8 2.0 fusion.82
  206.8 2.0 fusion.82
  208.9 2.0 fusion.82
  211.0 2.0 fusion.82
  213.0 2.0 fusion.82
  215.1 2.0 fusion.82
  217.1 1.7 while.76
  217.1 0.8 bitcast_dynamic-update-slice_fusion.2
  218.0 0.8 bitcast_dynamic-update-slice_fusion.2
  218.8 2.3 while.77
  218.8 1.1 fusion.75
  220.0 1.1 fusion.75
  221.1 0.6 copy-done.1
  221.8 7.6 %rev.6 = f32[8,512,512]{2,1,0:T(8,128)} reverse(f32[8,512,512]{2,1,0:T(8,128)} %get-tuple-element.945), dimensions={0} | reverse | bytes 16777216 | tf_op jit(solution)/shard_map/rev | solution.py:13
  229.4 0.6 dynamic-slice_bitcast_fusion
  230.0 30.4 %all-gather.15.cloned.1.call-done = f32[512,512]{1,0:T(8,128)} async-done(((f32[64,512]{1,0:T(8,128)}), f32[512,512]{1,0:T(8,128)}) %all-gather.15.cloned.1.call-update) | async-done | bytes 1048592 | tf_op jit(solution)/shard_map/all_gather | solution.py:11
  260.4 2.3 rev.7
  262.7 16.8 %while.80 = (s32[]{:T(128)}, f32[64,512]{1,0:T(8,128)S(1)}, s32[]{:T(128)}, f32[8,512,512]{2,1,0:T(8,128)}, f32[8,64,512]{2,1,0:T(8,128)}, /*index=5*/s32[]{:T(128)}, s32[]{:T(128)}) while((s32[]{:T(128)}, f32[64,512]{1,0:T(8,128)S(1)}, s32[]{:T(128)}, f32[8,512,512]{2,1,0:T(8,128)}, f32[8,64,512]{2,1,0:T(8,128)}, ...), condition=%wide.region_7.8_spmd.clone, body=%wide.region_6.7_spmd.clone.sunk | while | flops 201457664 | bytes 1837671 | solution.py:23
  262.7 2.4 fusion.85
  265.2 2.4 fusion.85
  267.6 2.4 fusion.85
  270.0 2.4 fusion.85
  272.4 2.4 fusion.85
  274.8 2.4 fusion.85
  277.2 2.4 fusion.85
  279.6 2.8 while.78
  279.9 1.1 fusion.78
  281.3 1.1 fusion.78
  282.4 0.6 copy-done.5
  (45 shorter events, 1.4 us)
Async XLA Ops:
  7.2 1.0 copy-start
  7.2 22.9 %all-gather.9.cloned.1.call-start = ((), (), s32[]{:S(2)}) async-start(), calls=%async_computation | async-start | bytes 1310720 | tf_op jit(solution)/shard_map/all_gather | solution.py:89
  10.5 66.9 %all-gather.13.cloned.1.call-start = ((), (), s32[]{:S(2)}) async-start(), calls=%async_computation.2 | async-start | bytes 1179648 | tf_op jit(solution)/shard_map/all_gather | solution.py:11
  20.0 0.8 copy-start.3
  34.0 1.2 copy-start.4
  36.9 165.8 %all-gather.11.cloned.1.call-start = ((), (), s32[]{:S(2)}) async-start(), calls=%async_computation.1 | async-start | bytes 9437184 | tf_op jit(solution)/shard_map/all_gather | solution.py:11
  42.7 217.7 %all-gather.15.cloned.1.call-start = ((), (), s32[]{:S(2)}) async-start(), calls=%async_computation.3 | async-start | bytes 1179648 | tf_op jit(solution)/shard_map/all_gather | solution.py:11
  221.1 0.6 copy-start.1
  262.7 16.9 %copy-start.2 = (f32[2,1,128,128]{3,2,1,0:T(8,128)S(1)}, f32[2,1,128,128]{3,2,1,0:T(8,128)}, u32[]{:S(2)}) copy-start(f32[2,1,128,128]{3,2,1,0:T(8,128)} %param.16) | copy-start | bytes 393220
  282.4 0.6 copy-start.5
Sparse Core Ops, SparseCore 0:
  10.6 19.4 all-gather.8
  37.0 40.2 all-gather.12
  79.5 123.1 all-gather.10
  221.9 38.4 all-gather.14
where the time goes:
time: 290 us
  waiting for transfers between devices  195 us (67%)
  matrix products  51.5 us (18%)
  local copies, waits for them, and re-layouts  21.4 us (7%)
  between operations  13.9 us (5%)
  blocking collectives  7.25 us (2%)
    all_gather x3, waiting for transfers between devices, carried_in(): pieces = jax.tree.map(lambda part: lax.all_gather(part, axis), value)  185 us
    dot_general x13, matrix products, matmul(): jnp.dot(left_side, right_factor, precision=PRECISE, preferred_element_typ...  23.7 us
    dot_general x11, matrix products, matmul_trans(): lax.dot_general(left_side, right_factor, (((1,), (1,)), ((), ())), precis...  21 us
    rev x2, local copies, waits for them, and re-layouts, carried_in(): pieces = jax.tree.map(lambda part: part[::-1], pieces)  9.88 us
    all_gather x1, waiting for transfers between devices, shards(): lax.all_gather(scaled, 'grp', axis=1, tiled=True)  9.25 us
    all_gather x1, blocking collectives, shards(): lax.all_gather(lifted, 'grp', axis=1, tiled=True)  7.25 us
  transfers between devices with their start and end apart: 4, of which 4 were waited for; matrix products, arithmetic and copies ran while one was open for 8% of the time, Pallas kernels for 0%

commit v1 on v0

--- a/solution.py
+++ b/solution.py
@@ -85,10 +85,21 @@
         precision=PRECISE,
         preferred_element_type=jnp.float32,
     )
-    blocks, offsets = (
-        lax.all_gather(scaled, "grp", axis=1, tiled=True),
-        lax.all_gather(lifted, "grp", axis=1, tiled=True),
-    )
+
+    def order_paths(panel):
+        y_new = lax.axis_size("grp")
+        response = lax.axis_index("grp")
+        reached, s_next = (y_new, response)
+        d_next, carry_out = (panel, 1)
+        while carry_out < reached:
+            current_arr = lax.ppermute(d_next, "grp", [(j, j ^ carry_out) for j in range(reached)])
+            met_up = jnp.concatenate([d_next, current_arr], axis=1)
+            k_now = jnp.concatenate([current_arr, d_next], axis=1)
+            d_next = jnp.where(s_next & carry_out == 0, met_up, k_now)
+            carry_out = 2 * carry_out
+        return d_next
+
+    blocks, offsets = (lax.all_gather(scaled, "grp", axis=1, tiled=True), order_paths(lifted))
     onehot = (pattern[..., None] == jnp.arange(groups, dtype=jnp.int32)).astype(jnp.float32)
     level_maps = -jnp.einsum(
         "lgkh,lgktj->lhjgt", onehot, blocks, precision=PRECISE, preferred_element_type=jnp.float32

time: 290 us -> 290 us (level)
  blocking collectives: 7.25 us -> 0 us
  starting transfers between devices: 0.34 us -> 3.82 us
  waiting for transfers between devices: 195 us -> 198 us
    all_gather x1 -> x0, blocking collectives: 7.25 us -> none  [shards(): lax.all_gather(lifted, 'grp', axis=1, tiled=True)]
    ppermute x0 -> x2, waiting for transfers between devices: none -> 3.95 us  [order_paths(): lax.ppermute(d_next, 'grp', [(j, j ^ carry_out) for j in range(reached)])]
    ppermute x0 -> x2, starting transfers between devices: none -> 3.48 us  [order_paths(): lax.ppermute(d_next, 'grp', [(j, j ^ carry_out) for j in range(reached)])]
  transfers between devices with their start and end apart: 4 -> 6, of which waited for: 4 -> 6; matrix products, arithmetic and copies ran while one was open for 8% -> 8% of each run, Pallas kernels for 0% -> 0%
where the time goes in v1:
time: 290 us
  waiting for transfers between devices  198 us (68%)
  matrix products  51.5 us (18%)
  local copies, waits for them, and re-layouts  21.3 us (7%)
  between operations  13.9 us (5%)
  starting transfers between devices  3.82 us (1%)
    all_gather x3, waiting for transfers between devices, carried_in(): pieces = jax.tree.map(lambda part: lax.all_gather(part, axis), value)  185 us
    dot_general x13, matrix products, matmul(): jnp.dot(left_side, right_factor, precision=PRECISE, preferred_element_typ...  23.7 us
    dot_general x11, matrix products, matmul_trans(): lax.dot_general(left_side, right_factor, (((1,), (1,)), ((), ())), precis...  21 us
    rev x2, local copies, waits for them, and re-layouts, carried_in(): pieces = jax.tree.map(lambda part: part[::-1], pieces)  9.88 us
    all_gather x1, waiting for transfers between devices, shards(): lax.all_gather(scaled, 'grp', axis=1, tiled=True)  8.38 us
  transfers between devices with their start and end apart: 6, of which 6 were waited for; matrix products, arithmetic and copies ran while one was open for 8% of the time, Pallas kernels for 0%

profile of v1, /device:TPU:0, one launch (start us, length us, event | category | flops | bytes accessed | tf_op | source)
XLA Modules:
  0.0 289.6 jit_solution(7165142452482208520)
XLA Ops:
  7.2 0.9 copy-done
  8.1 1.5 convolution_bitcast_fusion.4
  9.6 0.8 copy.22
  10.5 1.3 convolution_bitcast_fusion.5
  12.4 0.9 collective-permute-done
  13.3 2.9 %collective-permute-start.1 = (f32[2,2,64,128]{3,2,0,1:T(8,128)S(1)}, f32[2,2,64,128]{3,2,0,1:T(8,128)S(1)}, u32[]{:S(2)}, u32[]{:S(2)}) collective-permute-start(f32[2,2,64,128]{3,2,0,1:T(8,128)S(1)} %maximum_select_fusion.1), channel_id=1, source_target_pairs={{0,2},{1,3},{2,0},{3,1},{4,6},{5,7},{6,4},{7,5},{8,10},{9,11},{10,... | collective-permute-start | bytes 393224 | tf_op jit(solution)/shard_map/ppermute | solution.py:95
  16.2 0.8 copy.23
  17.0 3.0 %collective-permute-done.1 = f32[2,2,64,128]{3,2,0,1:T(8,128)S(1)} collective-permute-done((f32[2,2,64,128]{3,2,0,1:T(8,128)S(1)}, f32[2,2,64,128]{3,2,0,1:T(8,128)S(1)}, u32[]{:S(2)}, u32[]{:S(2)}) %collective-permute-start.1) | collective-permute-done | bytes 131104 | tf_op jit(solution)/shard_map/ppermute | solution.py:95
  20.0 0.8 fusion.47
  20.9 0.7 copy.25
  21.7 8.4 %all-gather.8.cloned.1.call-done = f32[2,4,2,128,128]{4,3,2,0,1:T(8,128)} async-done(((f32[2,1,2,128,128]{4,3,2,0,1:T(8,128)}), f32[2,4,2,128,128]{4,3,2,0,1:T(8,128)}) %all-gather.8.cloned.1.call-update) | async-done | bytes 1048592 | tf_op jit(solution)/shard_map/all_gather | solution.py:102
  30.0 3.9 %negate_bitcast_fusion = f32[2,4,128,4,128]{2,1,4,3,0:T(4,128)S(1)} fusion(f32[2,4,2,128,128]{4,3,2,0,1:T(8,128)} %all-gather.8.cloned.1.call-done, s32[2,4,2]{2,1,0:T(4,128)S(1)} %copy.23), kind=kOutput, calls=%fused_computation.46 | convolution fusion | flops 13107264 | bytes 3145792 | tf_op jit(solution)/shard_map/lgkh,lgktj->lhjgt/dot_general | solution.py:104
  34.0 1.2 fusion.58
  35.1 1.8 convolution_add_fusion
  37.0 5.7 %fusion.39 = f32[512,512]{1,0:T(8,128)} fusion(f32[64,8,4,128]{3,2,1,0:T(4,128)} %bitcast.160, f32[64,8,4,128]{3,2,1,0:T(4,128)S(1)} %bitcast.159), kind=kOutput, calls=%fused_computation.51 | convolution fusion | flops 1610612736 | bytes 3145728 | tf_op jit(solution)/shard_map/while/body/eval_jaxpr/dot_general | solution.py:27
  43.0 1.0 copy.59
  43.9 1.9 reshape.42
  45.8 1.9 copy.28
  47.7 29.6 %all-gather.12.cloned.1.call-done = f32[512,512]{1,0:T(8,128)} async-done(((f32[64,512]{1,0:T(8,128)}), f32[512,512]{1,0:T(8,128)}) %all-gather.12.cloned.1.call-update) | async-done | bytes 1048592 | tf_op jit(solution)/shard_map/all_gather | solution.py:11
  77.4 125.4 %all-gather.10.cloned.1.call-done = f32[4096,512]{1,0:T(8,128)} async-done(((f32[512,512]{1,0:T(8,128)}), f32[4096,512]{1,0:T(8,128)}) %all-gather.10.cloned.1.call-update) | async-done | bytes 8388624 | tf_op jit(solution)/shard_map/all_gather | solution.py:11
  202.7 14.4 %while.79 = (s32[]{:T(128)}, f32[64,512]{1,0:T(8,128)S(1)}, s32[]{:T(128)}, f32[8,512,512]{2,1,0:T(8,128)}, f32[8,64,512]{2,1,0:T(8,128)}, /*index=5*/s32[]{:T(128)}, s32[]{:T(128)}) while((s32[]{:T(128)}, f32[64,512]{1,0:T(8,128)S(1)}, s32[]{:T(128)}, f32[8,512,512]{2,1,0:T(8,128)}, f32[8,64,512]{2,1,0:T(8,128)}, ...), condition=%wide.region_1.2_spmd.clone, body=%wide.region_0.1_spmd.clone.sunk | while | flops 201457664 | bytes 1837671 | solution.py:23
  202.7 2.0 fusion.83
  204.8 2.0 fusion.83
  206.9 2.0 fusion.83
  208.9 2.0 fusion.83
  211.0 2.0 fusion.83
  213.0 2.0 fusion.83
  215.1 2.0 fusion.83
  217.1 1.7 while.76
  217.2 0.8 bitcast_dynamic-update-slice_fusion.2
  218.0 0.8 bitcast_dynamic-update-slice_fusion.2
  218.8 2.3 while.77
  218.9 1.1 fusion.76
  220.0 1.1 fusion.76
  221.8 7.6 %rev.6 = f32[8,512,512]{2,1,0:T(8,128)} reverse(f32[8,512,512]{2,1,0:T(8,128)} %get-tuple-element.947), dimensions={0} | reverse | bytes 16777216 | tf_op jit(solution)/shard_map/rev | solution.py:13
  230.0 30.4 %all-gather.14.cloned.1.call-done = f32[512,512]{1,0:T(8,128)} async-done(((f32[64,512]{1,0:T(8,128)}), f32[512,512]{1,0:T(8,128)}) %all-gather.14.cloned.1.call-update) | async-done | bytes 1048592 | tf_op jit(solution)/shard_map/all_gather | solution.py:11
  260.4 2.3 rev.7
  262.7 16.8 %while.80 = (s32[]{:T(128)}, f32[64,512]{1,0:T(8,128)S(1)}, s32[]{:T(128)}, f32[8,512,512]{2,1,0:T(8,128)}, f32[8,64,512]{2,1,0:T(8,128)}, /*index=5*/s32[]{:T(128)}, s32[]{:T(128)}) while((s32[]{:T(128)}, f32[64,512]{1,0:T(8,128)S(1)}, s32[]{:T(128)}, f32[8,512,512]{2,1,0:T(8,128)}, f32[8,64,512]{2,1,0:T(8,128)}, ...), condition=%wide.region_7.8_spmd.clone, body=%wide.region_6.7_spmd.clone.sunk | while | flops 201457664 | bytes 1837671 | solution.py:23
  262.7 2.4 fusion.86
  265.2 2.4 fusion.86
  267.6 2.4 fusion.86
  270.0 2.4 fusion.86
  272.4 2.4 fusion.86
  274.8 2.4 fusion.86
  277.2 2.4 fusion.86
  279.6 2.8 while.78
  279.9 1.1 fusion.79
  281.3 1.1 fusion.79
  (49 shorter events, 3.7 us)
Async XLA Ops:
  7.2 1.0 copy-start
  7.2 22.9 %all-gather.8.cloned.1.call-start = ((), (), s32[]{:S(2)}) async-start(), calls=%async_computation | async-start | bytes 1310720 | tf_op jit(solution)/shard_map/all_gather | solution.py:102
  10.5 66.9 %all-gather.12.cloned.1.call-start = ((), (), s32[]{:S(2)}) async-start(), calls=%async_computation.2 | async-start | bytes 1179648 | tf_op jit(solution)/shard_map/all_gather | solution.py:11
  11.8 1.5 collective-permute-start
  13.3 6.7 %collective-permute-start.1 = (f32[2,2,64,128]{3,2,0,1:T(8,128)S(1)}, f32[2,2,64,128]{3,2,0,1:T(8,128)S(1)}, u32[]{:S(2)}, u32[]{:S(2)}) collective-permute-start(f32[2,2,64,128]{3,2,0,1:T(8,128)S(1)} %maximum_select_fusion.1), channel_id=1, source_target_pairs={{0,2},{1,3},{2,0},{3,1},{4,6},{5,7},{6,4},{7,5},{8,10},{9,11},{10,... | collective-permute-start | bytes 393224 | tf_op jit(solution)/shard_map/ppermute | solution.py:95
  34.0 1.2 copy-start.3
  36.9 165.8 %all-gather.10.cloned.1.call-start = ((), (), s32[]{:S(2)}) async-start(), calls=%async_computation.1 | async-start | bytes 9437184 | tf_op jit(solution)/shard_map/all_gather | solution.py:11
  42.7 217.7 %all-gather.14.cloned.1.call-start = ((), (), s32[]{:S(2)}) async-start(), calls=%async_computation.3 | async-start | bytes 1179648 | tf_op jit(solution)/shard_map/all_gather | solution.py:11
  221.1 0.7 copy-start.1
  262.7 16.9 %copy-start.2 = (f32[2,1,128,128]{3,2,1,0:T(8,128)S(1)}, f32[2,1,128,128]{3,2,1,0:T(8,128)}, u32[]{:S(2)}) copy-start(f32[2,1,128,128]{3,2,1,0:T(8,128)} %param.16) | copy-start | bytes 393220
  282.4 0.6 copy-start.4
Sparse Core Ops, SparseCore 0:
  10.6 19.4 all-gather.7
  37.1 40.2 all-gather.11
  79.5 123.1 all-gather.9
  221.9 38.4 all-gather.13
